TPU v7x, 512 devices: a whole 4x8x8 slice. The times are simulated.
512 devices in a mesh: section: 32 (over z, x), et: 16 (over y, core).
Axes of the slice: x: 4, y: 8, z: 8, core: 2. Of those that a mesh axis runs over, the one named last changes fastest.
Arguments:
- x_fwd: bfloat16 [32, 256, 3072], P('section', 'et'), may hold values from -6 to 6
- act_fwd: bfloat16 [32, 256, 8192], P('section', None, 'et'), may hold values from -6 to 6
- ids_fwd: int32 [32, 256, 2], P('section'), may hold values from 0 to 7, as said below
- x_bwd: bfloat16 [32, 256, 3072], P('section', 'et'), may hold values from -6 to 6
- act_bwd: bfloat16 [32, 256, 8192], P('section', None, 'et'), may hold values from -6 to 6
- ids_bwd: int32 [32, 256, 2], P('section'), may hold values from 0 to 7, as said below
- grad_out: bfloat16 [32, 256, 3072], P('section', 'et'), may hold values from -6 to 6
- gain: bfloat16 [32, 3072], P('section'), may hold values from 0.099609375 to 1.8984375
- w_router: bfloat16 [32, 3072, 8], P('section'), may hold values from -0.21875 to 0.21875
- w_down: bfloat16 [32, 8192, 3072], P('section', 'et'), may hold values from -0.0625 to 0.0625
Outputs:
- fwd_in: bfloat16 [32, 256, 3072], P('section', 'et')
- incoming_gradient: bfloat16 [32, 256, 3072], P('section', 'et')
- dact: bfloat16 [32, 256, 8192], P('section', None, 'et')
Inputs may be any that keep to these rules, and one draw needn't show every extreme that they name: `ids_fwd`: each token names 2 different experts; in each section's micro-batch exactly 128 tokens name expert 0. `ids_bwd`: each token names 2 different experts; in each section's micro-batch exactly 128 tokens name expert 0.
All inputs are finite; a program needn't handle non-finite values.
Results may differ from a plain program's by a relative error of at most 0.014.
Values may be sent and summed in bfloat16 or wider, within the bound.
No kernel may reach another device: no remote copies, remote signals or barrier semaphores. Data moves between devices by JAX's collectives and lax.ppermute only.
A program may use at most 64 MiB of HBM per device.

v0:
```python
import jax
import jax.numpy as jnp
from jax import lax
from jax.sharding import PartitionSpec as P


def from_behind(value, axis, steps):
    count = lax.axis_size(axis)
    first, last = (max(0, -steps), min(count, count - steps))
    return lax.ppermute(value, axis, [(source, source + steps) for source in range(first, last)])


def norm_logits(inputs, gain, w_router):
    wide = inputs.astype(jnp.float32)
    inverse = lax.rsqrt(jnp.mean(wide * wide, axis=-1, keepdims=True) + 1e-05)
    normed = (wide * inverse * gain.astype(jnp.float32)).astype(jnp.bfloat16)
    logits = jnp.dot(normed, w_router, preferred_element_type=jnp.float32).astype(jnp.bfloat16)
    return (wide, inverse, logits)


def routing(logits, chosen, experts):
    route = jnp.sum((chosen == 0).astype(jnp.float32), axis=1)
    partner = jnp.minimum(jnp.sum(chosen, axis=1), experts - 1)
    labels = jnp.arange(experts, dtype=jnp.int32)
    onehot = (partner[:, None] == labels[None, :]).astype(jnp.float32)
    wide_logits = logits.astype(jnp.float32)
    sigma = jax.nn.sigmoid(wide_logits[:, 0] - jnp.sum(wide_logits * onehot, axis=1))
    return (route, onehot, sigma, route * sigma)


def arrange(chosen):
    member = jnp.sum((chosen == 0).astype(jnp.int32), axis=1)
    tally = jnp.sum(member)
    before = jnp.cumsum(member) - member
    after = jnp.cumsum(1 - member) - (1 - member)
    place = jnp.where(member == 1, before, tally + after)
    ordering = jnp.zeros_like(member).at[place].set(jnp.arange(member.shape[0], dtype=jnp.int32))
    return (member, place, ordering)


def spread_back(compact, member, place, capacity):
    safe = jnp.minimum(place, capacity - 1)
    return jnp.where(member[:, None] == 1, compact[safe], 0.0)


def shards(x_fwd, act_fwd, ids_fwd, x_bwd, act_bwd, ids_bwd, grad_out, gain, w_router, w_down):
    x_fwd, act_fwd, ids_fwd, x_bwd, act_bwd = (
        x_fwd[0],
        act_fwd[0],
        ids_fwd[0],
        x_bwd[0],
        act_bwd[0],
    )
    ids_bwd, grad_out, gain, w_router, w_down = (
        ids_bwd[0],
        grad_out[0],
        gain[0],
        w_router[0],
        w_down[0],
    )
    experts = w_router.shape[1]
    tokens = ids_fwd.shape[0]
    capacity = tokens // 2
    own_rows = x_fwd.shape[0]
    first_row = lax.axis_index("et") * own_rows
    wide_f, inverse_f, logit_f = norm_logits(x_fwd, gain, w_router)
    backward_wide_rows, backward_inverse_norm, logit_b = norm_logits(x_bwd, gain, w_router)
    full_f, full_b, full_g = (
        lax.all_gather(logit_f, "et", axis=0, tiled=True),
        lax.all_gather(logit_b, "et", axis=0, tiled=True),
        lax.all_gather(grad_out, "et", axis=0, tiled=True),
    )
    route_f, onehot_f, sigma_f, coef_f = routing(full_f, ids_fwd, experts)
    member_f, place_f, order_f = arrange(ids_fwd)
    chosen_f = order_f[:capacity]
    compact = (
        jnp.dot(act_fwd[chosen_f], w_down, preferred_element_type=jnp.float32)
        * coef_f[chosen_f][:, None]
    )
    summed = lax.psum(compact.astype(jnp.bfloat16), "et").astype(jnp.float32)
    member_own = lax.dynamic_slice_in_dim(member_f, first_row, own_rows, 0)
    place_own = lax.dynamic_slice_in_dim(place_f, first_row, own_rows, 0)
    y_mine = spread_back(summed, member_own, place_own, capacity)
    layer_out = (wide_f + y_mine).astype(jnp.bfloat16)
    route_b, onehot_b, sigma_b, backward_coefficient = routing(full_b, ids_bwd, experts)
    member_b, place_b, order_b = arrange(ids_bwd)
    chosen_b = order_b[:capacity]
    up_compact = lax.dot_general(
        full_g[chosen_b], w_down, (((1,), (1,)), ((), ())), preferred_element_type=jnp.float32
    )
    back_up = spread_back(up_compact, member_b, place_b, capacity)
    dact = (backward_coefficient[:, None] * back_up).astype(jnp.bfloat16)
    dprob_part = jnp.sum(act_bwd.astype(jnp.float32) * back_up, axis=1)
    dprob_all = lax.psum(dprob_part, "et")
    dprob_mine = lax.dynamic_slice_in_dim(dprob_all, first_row, own_rows, 0)
    route_mine = lax.dynamic_slice_in_dim(route_b, first_row, own_rows, 0)
    sigma_mine = lax.dynamic_slice_in_dim(sigma_b, first_row, own_rows, 0)
    onehot_mine = lax.dynamic_slice_in_dim(onehot_b, first_row, own_rows, 0)
    slope = route_mine * dprob_mine * sigma_mine * (1.0 - sigma_mine)
    router_wide = w_router.astype(jnp.float32)
    spread = router_wide[:, 0][None, :] - jnp.dot(
        onehot_mine, router_wide.T, precision=lax.Precision.HIGHEST
    )
    dnormed = slope[:, None] * spread
    scaled_rows = dnormed * gain.astype(jnp.float32)
    normalized_input = backward_wide_rows * backward_inverse_norm
    norm_input_gradient = backward_inverse_norm * (
        scaled_rows
        - normalized_input * jnp.mean(scaled_rows * normalized_input, axis=-1, keepdims=True)
    )
    input_grad = (grad_out.astype(jnp.float32) + norm_input_gradient).astype(jnp.bfloat16)
    fwd_in = from_behind(layer_out, "section", 1)
    incoming_gradient = from_behind(input_grad, "section", -1)
    return (fwd_in[None], incoming_gradient[None], dact[None])


def solution(mesh):
    placed = (
        P("section", "et", None),
        P("section", None, "et"),
        P("section", None, None),
        P("section", "et", None),
        P("section", None, "et"),
        P("section", None, None),
        P("section", "et", None),
        P("section", None),
        P("section", None, None),
        P("section", "et", None),
    )
    return jax.shard_map(
        shards,
        mesh=mesh,
        in_specs=placed,
        out_specs=(P("section", "et", None), P("section", "et", None), P("section", None, "et")),
        check_vma=False,
    )
```

profile of v0, /device:TPU:6, one launch (start us, length us, event | category | flops | bytes accessed | tf_op | source)
XLA Modules:
  0.0 256.7 jit_solution(1746351903962819599)
XLA Ops:
  7.2 0.9 convert_reduce_fusion.5
  8.1 1.4 convert_reduce_fusion
  9.5 0.3 reduce-window.34
  10.6 0.7 compare_select_fusion.8
  11.3 0.7 compare_select_fusion.2
  11.9 1.4 scatter_custom_fusion
  13.4 0.7 mul.173
  14.1 1.0 fusion.22
  15.1 1.1 fusion.6
  16.3 17.6 %all-gather.1 = bf16[16,16,8]{1,2,0:T(8,128)(2,1)S(1)} all-gather(bf16[1,16,8]{1,2,0:T(8,128)(2,1)S(1)} %fusion.6), channel_id=1, replica_groups=mesh['section'=32,'et'=16] {'et'}, dimensions={0}, use_global_device_ids=true | all-gather | bytes 4352 | tf_op jit(solution)/shard_map/all_gather | solution.py:69
  34.1 1.9 gather_fusion
  36.0 1.3 gather_fusion.1
  37.3 1.5 fusion
  38.8 0.7 all-gather.5.cloned.1.call-update
  39.6 0.6 pad_clamp_fusion.2
  40.4 1.0 fusion.7
  41.4 0.3 reduce-window.50
  42.0 0.3 reduce-window.48
  42.6 1.2 compare_select_fusion
  43.8 1.4 scatter_custom_fusion.1
  45.3 0.7 dynamic-slice_compare_fusion
  45.9 15.0 %all-gather.2 = bf16[16,16,8]{1,2,0:T(8,128)(2,1)S(1)} all-gather(bf16[1,16,8]{1,2,0:T(8,128)(2,1)S(1)} %fusion.7), channel_id=1, replica_groups=mesh['section'=32,'et'=16] {'et'}, dimensions={0}, use_global_device_ids=true | all-gather | bytes 4352 | tf_op jit(solution)/shard_map/all_gather | solution.py:70
  61.0 0.6 pad_clamp_fusion.1
  61.7 0.6 broadcast_compare_fusion.2
  62.2 0.6 iota_compare_fusion
  62.8 0.6 divide_multiply_fusion
  63.4 0.6 add_divide_fusion
  63.9 1.4 slice_convert_fusion
  65.3 92.2 %all-reduce.2.cloned.1.call-done = bf16[128,3072]{1,0:T(8,128)(2,1)} async-done(((bf16[128,3072]{1,0:T(8,128)(2,1)}), bf16[128,3072]{1,0:T(8,128)(2,1)}) %all-reduce.2.cloned.1.call-update) | async-done | bytes 786448 | tf_op jit(solution)/shard_map/psum | solution.py:80
  157.6 2.4 convert_element_type.106
  160.0 2.2 gather_fusion.2
  162.2 0.8 fusion.23
  163.0 3.5 %collective-permute-start = (bf16[16,3072]{1,0:T(8,128)(2,1)S(1)}, bf16[16,3072]{1,0:T(8,128)(2,1)}, u32[]{:S(2)}, u32[]{:S(2)}) collective-permute-start(bf16[16,3072]{1,0:T(8,128)(2,1)S(1)} %fusion.23), channel_id=1, source_target_pairs={{0,16},{16,32},{32,48},{48,64},{64,80},{80,96},{96,112},{112,128},... | collective-permute-start | bytes 294920 | tf_op jit(solution)/shard_map/ppermute | solution.py:10
  166.5 0.6 pad_clamp_fusion
  167.2 2.4 collective-permute-done
  169.6 32.3 %all-gather.5.cloned.1.call-done = bf16[1,256,3072]{2,1,0:T(8,128)(2,1)} async-done(((bf16[1,16,3072]{2,1,0:T(8,128)(2,1)}), bf16[1,256,3072]{2,1,0:T(8,128)(2,1)}) %all-gather.5.cloned.1.call-update) | async-done | bytes 1572880 | tf_op jit(solution)/shard_map/all_gather | solution.py:71
  201.9 4.5 %gather_fusion.3 = bf16[128,3072]{1,0:T(8,128)(2,1)} fusion(bf16[256,3072]{1,0:T(8,128)(2,1)} %bitcast.108, s32[1024]{0:T(1024)} %pad_clamp_fusion.1), kind=kCustom, calls=%fused_computation.3 | custom fusion | bytes 1573376 | tf_op jit(solution)/shard_map/gather | solution.py:89
  206.3 2.3 fusion.3
  208.7 1.8 gather_fusion.4
  210.5 1.3 fusion.8
  211.8 24.9 %psum.15 = f32[256]{0:T(256)S(1)} all-reduce(f32[256]{0:T(256)S(1)} %fusion.8), channel_id=1, replica_groups=mesh['section'=32,'et'=16] {'et'}, use_global_device_ids=true, to_apply=%region_22.23 | all-reduce | flops 256 | bytes 2048 | tf_op jit(solution)/shard_map/psum | solution.py:94
  236.8 1.2 fusion.17
  238.0 1.0 fusion.21
  239.0 2.8 %collective-permute-start.1 = (bf16[16,3072]{1,0:T(8,128)(2,1)S(1)}, bf16[16,3072]{1,0:T(8,128)(2,1)S(1)}, u32[]{:S(2)}, u32[]{:S(2)}) collective-permute-start(bf16[16,3072]{1,0:T(8,128)(2,1)S(1)} %fusion.21), channel_id=1, source_target_pairs={{16,0},{32,16},{48,32},{64,48},{80,64},{96,80},{112,96},{128,112},... | collective-permute-start | bytes 294920 | tf_op jit(solution)/shard_map/ppermute | solution.py:10
  241.8 1.9 fusion.10
  243.7 4.0 %collective-permute-done.1 = bf16[16,3072]{1,0:T(8,128)(2,1)S(1)} collective-permute-done((bf16[16,3072]{1,0:T(8,128)(2,1)S(1)}, bf16[16,3072]{1,0:T(8,128)(2,1)S(1)}, u32[]{:S(2)}, u32[]{:S(2)}) %collective-permute-start.1) | collective-permute-done | bytes 98336 | tf_op jit(solution)/shard_map/ppermute | solution.py:10
  247.6 1.5 copy.20
  249.2 0.6 copy.21
  (63 shorter events, 2.1 us)
Async XLA Ops:
  7.2 30.1 %copy-start = (bf16[1,512,3072]{2,1,0:T(8,128)(2,1)S(1)}, bf16[1,512,3072]{2,1,0:T(8,128)(2,1)}, u32[]{:S(2)}) copy-start(bf16[1,512,3072]{2,1,0:T(8,128)(2,1)} %param.19) | copy-start | bytes 9437188
  7.2 150.4 %all-reduce.2.cloned.1.call-start = ((), (), s32[]{:S(2)}) async-start(), calls=%async_computation | async-start | bytes 1572864 | tf_op jit(solution)/shard_map/psum | solution.py:80
  34.0 6.2 %copy-start.2 = (bf16[1,16,3072]{2,1,0:T(8,128)(2,1)S(1)}, bf16[1,16,3072]{2,1,0:T(8,128)(2,1)}, u32[]{:S(2)}) copy-start(bf16[1,16,3072]{2,1,0:T(8,128)(2,1)} %param.13) | copy-start | bytes 294916
  35.9 25.7 %copy-start.4 = (s32[1,256,2]{1,2,0:T(2,128)S(1)}, s32[1,256,2]{1,2,0:T(2,128)}, u32[]{:S(2)}) copy-start(s32[1,256,2]{1,2,0:T(2,128)} %param.15) | copy-start | bytes 6148
  38.8 123.5 %copy-start.1 = (bf16[1,16,3072]{2,1,0:T(8,128)(2,1)S(1)}, bf16[1,16,3072]{2,1,0:T(8,128)(2,1)}, u32[]{:S(2)}) copy-start(bf16[1,16,3072]{2,1,0:T(8,128)(2,1)} %param.10) | copy-start | bytes 294916
  38.8 163.1 %all-gather.5.cloned.1.call-start = ((), (), s32[]{:S(2)}) async-start(), calls=%async_computation.1 | async-start | bytes 1671168 | tf_op jit(solution)/shard_map/all_gather | solution.py:71
  40.4 1.0 copy-start.9
  163.0 6.6 %collective-permute-start = (bf16[16,3072]{1,0:T(8,128)(2,1)S(1)}, bf16[16,3072]{1,0:T(8,128)(2,1)}, u32[]{:S(2)}, u32[]{:S(2)}) collective-permute-start(bf16[16,3072]{1,0:T(8,128)(2,1)S(1)} %fusion.23), channel_id=1, source_target_pairs={{0,16},{16,32},{32,48},{48,64},{64,80},{80,96},{96,112},{112,128},... | collective-permute-start | bytes 294920 | tf_op jit(solution)/shard_map/ppermute | solution.py:10
  208.7 1.8 copy-start.8
  208.7 28.0 %copy-start.6 = (f32[256]{0:T(256)S(1)}, f32[256]{0:T(256)}, u32[]{:S(2)}) copy-start(f32[256]{0:T(256)} %add_divide_fusion) | copy-start | bytes 3076
  208.7 28.1 %copy-start.3 = (f32[3072,1]{0,1:T(1,128)S(1)}, f32[3072,1]{0,1:T(1,128)}, u32[]{:S(2)}) copy-start(f32[3072,1]{0,1:T(1,128)} %slice_convert_fusion) | copy-start | bytes 36868
  208.7 28.1 %copy-start.7 = (pred[256,8]{0,1:T(8,128)(4,1)S(1)}, pred[256,8]{0,1:T(8,128)(4,1)}, u32[]{:S(2)}) copy-start(pred[256,8]{0,1:T(8,128)(4,1)} %iota_compare_fusion) | copy-start | bytes 6148
  208.7 33.1 %copy-start.5 = (f32[256,1]{0,1:T(1,128)S(1)}, f32[256,1]{0,1:T(1,128)}, u32[]{:S(2)}) copy-start(f32[256,1]{0,1:T(1,128)} %get-tuple-element.14) | copy-start | bytes 3076
  239.0 8.6 %collective-permute-start.1 = (bf16[16,3072]{1,0:T(8,128)(2,1)S(1)}, bf16[16,3072]{1,0:T(8,128)(2,1)S(1)}, u32[]{:S(2)}, u32[]{:S(2)}) collective-permute-start(bf16[16,3072]{1,0:T(8,128)(2,1)S(1)} %fusion.21), channel_id=1, source_target_pairs={{16,0},{32,16},{48,32},{64,48},{80,64},{96,80},{112,96},{128,112},... | collective-permute-start | bytes 294920 | tf_op jit(solution)/shard_map/ppermute | solution.py:10
Sparse Core Ops, SparseCore 0:
  38.9 118.5 all-reduce.1
  159.7 42.1 all-gather.4
where the time goes:
time: 257 us
  waiting for transfers between devices  132 us (51%)
  blocking collectives  57.5 us (22%)
  other arithmetic  22.1 us (9%)
  local copies, waits for them, and re-layouts  17.6 us (7%)
  between operations  14.3 us (6%)
  matrix products  7.15 us (3%)
  starting transfers between devices  6.38 us (2%)
    psum x1, waiting for transfers between devices, shards(): summed = lax.psum(compact.astype(jnp.bfloat16), 'et').astype(jnp.float32)  92.2 us
    all_gather x1, waiting for transfers between devices, shards(): lax.all_gather(grad_out, 'et', axis=0, tiled=True)  32.3 us
    psum x1, blocking collectives, shards(): dprob_all = lax.psum(dprob_part, 'et')  24.9 us
    all_gather x1, blocking collectives, shards(): lax.all_gather(logit_f, 'et', axis=0, tiled=True)  17.6 us
    all_gather x1, blocking collectives, shards(): lax.all_gather(logit_b, 'et', axis=0, tiled=True)  15 us
    ppermute x2, waiting for transfers between devices, from_behind(): lax.ppermute(value, axis, [(source, source + steps) for source in range(f...  6.38 us
    ppermute x2, starting transfers between devices, from_behind(): lax.ppermute(value, axis, [(source, source + steps) for source in range(f...  6.3 us
  transfers between devices with their start and end apart: 4, of which 4 were waited for; matrix products, arithmetic and copies ran while one was open for 7% of the time, Pallas kernels for 0%

commit v1 on v0

--- a/solution.py
+++ b/solution.py
@@ -91,7 +91,7 @@
     back_up = spread_back(up_compact, member_b, place_b, capacity)
     dact = (backward_coefficient[:, None] * back_up).astype(jnp.bfloat16)
     dprob_part = jnp.sum(act_bwd.astype(jnp.float32) * back_up, axis=1)
-    dprob_all = lax.psum(dprob_part, "et")
+    dprob_all = jnp.sum(lax.all_gather(dprob_part, "et"), axis=0)
     dprob_mine = lax.dynamic_slice_in_dim(dprob_all, first_row, own_rows, 0)
     route_mine = lax.dynamic_slice_in_dim(route_b, first_row, own_rows, 0)
     sigma_mine = lax.dynamic_slice_in_dim(sigma_b, first_row, own_rows, 0)

time: 257 us -> 249 us (0.969)
  blocking collectives: 57.5 us -> 48.3 us
    psum x1 -> x0, blocking collectives: 24.9 us -> none  [shards(): dprob_all = lax.psum(dprob_part, 'et')]
    all_gather x0 -> x1, blocking collectives: none -> 15.7 us  [shards(): dprob_all = jnp.sum(lax.all_gather(dprob_part, 'et'), axis=0)]
  transfers between devices with their start and end apart: 4 -> 4, of which waited for: 4 -> 4; matrix products, arithmetic and copies ran while one was open for 7% -> 8% of each run, Pallas kernels for 0% -> 0%
where the time goes in v1:
time: 249 us; the launch traced here: 248 us
  waiting for transfers between devices  132 us (53%)
  blocking collectives  48.3 us (19%)
  other arithmetic  22.2 us (9%)
  local copies, waits for them, and re-layouts  17.6 us (7%)
  between operations  14.3 us (6%)
  matrix products  7.15 us (3%)
  starting transfers between devices  6.38 us (3%)
    psum x1, waiting for transfers between devices, shards(): summed = lax.psum(compact.astype(jnp.bfloat16), 'et').astype(jnp.float32)  92.2 us
    all_gather x1, waiting for transfers between devices, shards(): lax.all_gather(grad_out, 'et', axis=0, tiled=True)  32.3 us
    all_gather x1, blocking collectives, shards(): lax.all_gather(logit_f, 'et', axis=0, tiled=True)  17.6 us
    all_gather x1, blocking collectives, shards(): dprob_all = jnp.sum(lax.all_gather(dprob_part, 'et'), axis=0)  15.7 us
    all_gather x1, blocking collectives, shards(): lax.all_gather(logit_b, 'et', axis=0, tiled=True)  15 us
    ppermute x2, waiting for transfers between devices, from_behind(): lax.ppermute(value, axis, [(source, source + steps) for source in range(f...  6.82 us
    ppermute x2, starting transfers between devices, from_behind(): lax.ppermute(value, axis, [(source, source + steps) for source in range(f...  6.3 us
  transfers between devices with their start and end apart: 4, of which 4 were waited for; matrix products, arithmetic and copies ran while one was open for 8% of the time, Pallas kernels for 0%

profile of v1, /device:TPU:6, one launch (start us, length us, event | category | flops | bytes accessed | tf_op | source)
XLA Modules:
  0.0 247.9 jit_solution(7735916414955716565)
XLA Ops:
  7.2 0.9 convert_reduce_fusion.5
  8.1 1.4 convert_reduce_fusion
  9.5 0.3 reduce-window.34
  10.6 0.7 compare_select_fusion.8
  11.3 0.7 compare_select_fusion.2
  11.9 1.4 scatter_custom_fusion
  13.4 0.7 mul.173
  14.1 1.0 fusion.22
  15.1 1.1 fusion.6
  16.3 17.6 %all-gather.2 = bf16[16,16,8]{1,2,0:T(8,128)(2,1)S(1)} all-gather(bf16[1,16,8]{1,2,0:T(8,128)(2,1)S(1)} %fusion.6), channel_id=1, replica_groups=mesh['section'=32,'et'=16] {'et'}, dimensions={0}, use_global_device_ids=true | all-gather | bytes 4352 | tf_op jit(solution)/shard_map/all_gather | solution.py:69
  34.1 1.9 gather_fusion
  36.0 1.3 gather_fusion.1
  37.3 1.5 fusion
  38.8 0.7 all-gather.7.cloned.1.call-update
  39.6 0.6 pad_clamp_fusion.2
  40.4 1.0 fusion.7
  41.4 0.3 reduce-window.50
  42.0 0.3 reduce-window.48
  42.6 1.2 compare_select_fusion
  43.8 1.4 scatter_custom_fusion.1
  45.3 0.7 dynamic-slice_compare_fusion
  45.9 15.0 %all-gather.4 = bf16[16,16,8]{1,2,0:T(8,128)(2,1)S(1)} all-gather(bf16[1,16,8]{1,2,0:T(8,128)(2,1)S(1)} %fusion.7), channel_id=1, replica_groups=mesh['section'=32,'et'=16] {'et'}, dimensions={0}, use_global_device_ids=true | all-gather | bytes 4352 | tf_op jit(solution)/shard_map/all_gather | solution.py:70
  61.0 0.6 pad_clamp_fusion.1
  61.7 0.6 broadcast_compare_fusion.2
  62.2 0.6 iota_compare_fusion
  62.8 0.6 divide_multiply_fusion
  63.4 0.6 add_divide_fusion
  63.9 1.4 slice_convert_fusion
  65.3 92.2 %all-reduce.2.cloned.1.call-done = bf16[128,3072]{1,0:T(8,128)(2,1)} async-done(((bf16[128,3072]{1,0:T(8,128)(2,1)}), bf16[128,3072]{1,0:T(8,128)(2,1)}) %all-reduce.2.cloned.1.call-update) | async-done | bytes 786448 | tf_op jit(solution)/shard_map/psum | solution.py:80
  157.6 2.4 convert_element_type.106
  160.0 2.2 gather_fusion.2
  162.2 0.8 fusion.23
  163.0 3.5 %collective-permute-start = (bf16[16,3072]{1,0:T(8,128)(2,1)S(1)}, bf16[16,3072]{1,0:T(8,128)(2,1)}, u32[]{:S(2)}, u32[]{:S(2)}) collective-permute-start(bf16[16,3072]{1,0:T(8,128)(2,1)S(1)} %fusion.23), channel_id=1, source_target_pairs={{0,16},{16,32},{32,48},{48,64},{64,80},{80,96},{96,112},{112,128},... | collective-permute-start | bytes 294920 | tf_op jit(solution)/shard_map/ppermute | solution.py:10
  166.5 0.6 pad_clamp_fusion
  167.2 2.4 collective-permute-done
  169.6 32.3 %all-gather.7.cloned.1.call-done = bf16[1,256,3072]{2,1,0:T(8,128)(2,1)} async-done(((bf16[1,16,3072]{2,1,0:T(8,128)(2,1)}), bf16[1,256,3072]{2,1,0:T(8,128)(2,1)}) %all-gather.7.cloned.1.call-update) | async-done | bytes 1572880 | tf_op jit(solution)/shard_map/all_gather | solution.py:71
  201.9 4.5 %gather_fusion.3 = bf16[128,3072]{1,0:T(8,128)(2,1)} fusion(bf16[256,3072]{1,0:T(8,128)(2,1)} %bitcast.109, s32[1024]{0:T(1024)} %pad_clamp_fusion.1), kind=kCustom, calls=%fused_computation.3 | custom fusion | bytes 1573376 | tf_op jit(solution)/shard_map/gather | solution.py:89
  206.3 2.3 fusion.3
  208.7 1.8 gather_fusion.4
  210.5 1.3 fusion.8
  211.8 15.7 %all-gather.3 = f32[16,1,256]{2,1,0:T(1,128)S(1)} all-gather(f32[1,1,256]{2,1,0:T(1,128)S(1)} %bitcast.123), channel_id=3, replica_groups=mesh['section'=32,'et'=16] {'et'}, dimensions={0}, use_global_device_ids=true | all-gather | bytes 17408 | tf_op jit(solution)/shard_map/all_gather | solution.py:94
  227.6 1.2 fusion.17
  228.8 1.0 fusion.21
  229.8 2.8 %collective-permute-start.1 = (bf16[16,3072]{1,0:T(8,128)(2,1)S(1)}, bf16[16,3072]{1,0:T(8,128)(2,1)S(1)}, u32[]{:S(2)}, u32[]{:S(2)}) collective-permute-start(bf16[16,3072]{1,0:T(8,128)(2,1)S(1)} %fusion.21), channel_id=1, source_target_pairs={{16,0},{32,16},{48,32},{64,48},{80,64},{96,80},{112,96},{128,112},... | collective-permute-start | bytes 294920 | tf_op jit(solution)/shard_map/ppermute | solution.py:10
  232.6 1.9 fusion.10
  234.5 4.4 %collective-permute-done.1 = bf16[16,3072]{1,0:T(8,128)(2,1)S(1)} collective-permute-done((bf16[16,3072]{1,0:T(8,128)(2,1)S(1)}, bf16[16,3072]{1,0:T(8,128)(2,1)S(1)}, u32[]{:S(2)}, u32[]{:S(2)}) %collective-permute-start.1) | collective-permute-done | bytes 98336 | tf_op jit(solution)/shard_map/ppermute | solution.py:10
  238.9 1.5 copy.20
  240.4 0.6 copy.21
  (64 shorter events, 2.2 us)
Async XLA Ops:
  7.2 30.1 %copy-start = (bf16[1,512,3072]{2,1,0:T(8,128)(2,1)S(1)}, bf16[1,512,3072]{2,1,0:T(8,128)(2,1)}, u32[]{:S(2)}) copy-start(bf16[1,512,3072]{2,1,0:T(8,128)(2,1)} %param.19) | copy-start | bytes 9437188
  7.2 150.4 %all-reduce.2.cloned.1.call-start = ((), (), s32[]{:S(2)}) async-start(), calls=%async_computation | async-start | bytes 1572864 | tf_op jit(solution)/shard_map/psum | solution.py:80
  34.0 6.2 %copy-start.2 = (bf16[1,16,3072]{2,1,0:T(8,128)(2,1)S(1)}, bf16[1,16,3072]{2,1,0:T(8,128)(2,1)}, u32[]{:S(2)}) copy-start(bf16[1,16,3072]{2,1,0:T(8,128)(2,1)} %param.13) | copy-start | bytes 294916
  35.9 25.7 %copy-start.4 = (s32[1,256,2]{1,2,0:T(2,128)S(1)}, s32[1,256,2]{1,2,0:T(2,128)}, u32[]{:S(2)}) copy-start(s32[1,256,2]{1,2,0:T(2,128)} %param.15) | copy-start | bytes 6148
  38.8 123.5 %copy-start.1 = (bf16[1,16,3072]{2,1,0:T(8,128)(2,1)S(1)}, bf16[1,16,3072]{2,1,0:T(8,128)(2,1)}, u32[]{:S(2)}) copy-start(bf16[1,16,3072]{2,1,0:T(8,128)(2,1)} %param.10) | copy-start | bytes 294916
  38.8 163.1 %all-gather.7.cloned.1.call-start = ((), (), s32[]{:S(2)}) async-start(), calls=%async_computation.1 | async-start | bytes 1671168 | tf_op jit(solution)/shard_map/all_gather | solution.py:71
  40.4 1.0 copy-start.9
  163.0 6.6 %collective-permute-start = (bf16[16,3072]{1,0:T(8,128)(2,1)S(1)}, bf16[16,3072]{1,0:T(8,128)(2,1)}, u32[]{:S(2)}, u32[]{:S(2)}) collective-permute-start(bf16[16,3072]{1,0:T(8,128)(2,1)S(1)} %fusion.23), channel_id=1, source_target_pairs={{0,16},{16,32},{32,48},{48,64},{64,80},{80,96},{96,112},{112,128},... | collective-permute-start | bytes 294920 | tf_op jit(solution)/shard_map/ppermute | solution.py:10
  208.7 1.8 copy-start.8
  208.7 18.9 %copy-start.6 = (f32[256]{0:T(256)S(1)}, f32[256]{0:T(256)}, u32[]{:S(2)}) copy-start(f32[256]{0:T(256)} %add_divide_fusion) | copy-start | bytes 3076
  208.7 18.9 %copy-start.3 = (f32[3072,1]{0,1:T(1,128)S(1)}, f32[3072,1]{0,1:T(1,128)}, u32[]{:S(2)}) copy-start(f32[3072,1]{0,1:T(1,128)} %slice_convert_fusion) | copy-start | bytes 36868
  208.7 18.9 %copy-start.7 = (pred[256,8]{0,1:T(8,128)(4,1)S(1)}, pred[256,8]{0,1:T(8,128)(4,1)}, u32[]{:S(2)}) copy-start(pred[256,8]{0,1:T(8,128)(4,1)} %iota_compare_fusion) | copy-start | bytes 6148
  208.7 23.9 %copy-start.5 = (f32[256,1]{0,1:T(1,128)S(1)}, f32[256,1]{0,1:T(1,128)}, u32[]{:S(2)}) copy-start(f32[256,1]{0,1:T(1,128)} %get-tuple-element.14) | copy-start | bytes 3076
  229.8 9.0 %collective-permute-start.1 = (bf16[16,3072]{1,0:T(8,128)(2,1)S(1)}, bf16[16,3072]{1,0:T(8,128)(2,1)S(1)}, u32[]{:S(2)}, u32[]{:S(2)}) collective-permute-start(bf16[16,3072]{1,0:T(8,128)(2,1)S(1)} %fusion.21), channel_id=1, source_target_pairs={{16,0},{32,16},{48,32},{64,48},{80,64},{96,80},{112,96},{128,112},... | collective-permute-start | bytes 294920 | tf_op jit(solution)/shard_map/ppermute | solution.py:10
Sparse Core Ops, SparseCore 0:
  38.9 118.5 all-reduce.1
  159.7 42.1 all-gather.6
